TPU v7x, 512 devices: a whole 4x8x8 slice. The times are simulated.
512 devices in a mesh: section: 8 (over z), ctx: 8 (over y_hi, x), tp: 8 (over y_lo, core).
Axes of the slice: x: 4, y: 8 (y_hi: 2, y_lo: 4; y = y_hi * 4 + y_lo), z: 8, core: 2. Of those that a mesh axis runs over, the one named last changes fastest.
Arguments:
- block_order: int32 [16], replicated, may hold values from 0 to 15, each once
- plan: int32 [8], replicated, may hold values from 0 to 1
- q_box: bfloat16 [8, 2, 1408, 8192], P('section', None, 'ctx', 'tp'), may hold values from -8 to 8
- k_box: bfloat16 [8, 2, 1408, 1024], P('section', None, ('ctx', 'tp')), may hold values from -8 to 8
- v_box: bfloat16 [8, 2, 1408, 1024], P('section', None, ('ctx', 'tp')), may hold values from -6 to 6
- grad_out: bfloat16 [8, 1408, 8192], P('section', 'ctx', 'tp'), may hold values from -6 to 6
Outputs:
- attn_out: bfloat16 [8, 1408, 8192], P('section', 'ctx', 'tp')
- grad_q: bfloat16 [8, 1408, 8192], P('section', 'ctx', 'tp')
- grad_k: float32 [8, 1408, 1024], P('section', ('ctx', 'tp'))
- grad_v: float32 [8, 1408, 1024], P('section', ('ctx', 'tp'))
Inputs may be any that keep to these rules, and one draw needn't show every extreme that they name: `block_order`: a permutation: every block sits in exactly one storage slot, slot j covering storage rows j * 88 to (j + 1) * 88 - 1.
All inputs are finite; a program needn't handle non-finite values.
Results may differ from a plain program's by a relative error of at most 0.012.
Values may be sent and summed in bfloat16 or wider, within the bound.
No kernel may reach another device: no remote copies, remote signals or barrier semaphores. Data moves between devices by JAX's collectives and lax.ppermute only.
A program may use at most 64 MiB of HBM per device.

v0:
```python
import jax
import jax.numpy as jnp
from jax import lax
from jax.sharding import PartitionSpec as P

HEAD_DIM = 128
NEG = -1e30


def passed_along(block, axis, distance):
    devices = range(lax.axis_size(axis))
    route = [((i - distance) % len(devices), i) for i in devices]
    return lax.ppermute(block, axis, route)


def body(block_order, plan, q_box, k_box, v_box, grad_out):
    tp_count = lax.axis_size("tp")
    ctx_count = lax.axis_size("ctx")
    tok_rows = q_box.shape[2]
    seq_rows = tok_rows * ctx_count
    block_len = tok_rows // 2
    head_size = HEAD_DIM
    heads_local = q_box.shape[3] // head_size
    kv_local = k_box.shape[3] // head_size // tp_count
    group = heads_local // kv_local
    kv_width = kv_local * head_size
    scale = head_size ** (-0.5)
    section_rank = lax.axis_index("section")
    tp_rank = lax.axis_index("tp")
    arrived = passed_along((q_box[0], k_box[0], v_box[0]), "section", 1)
    wanted = lax.dynamic_index_in_dim(plan, section_rank, 0, keepdims=False)
    queries = lax.dynamic_index_in_dim(arrived[0], wanted, 0, keepdims=False)
    key_rows = lax.dynamic_index_in_dim(arrived[1], wanted, 0, keepdims=False)
    value_rows = lax.dynamic_index_in_dim(arrived[2], wanted, 0, keepdims=False)
    cotangent = passed_along(grad_out[0], "section", -1)
    positions = (
        block_order[:, None] * block_len + jnp.arange(block_len, dtype=jnp.int32)[None, :]
    ).reshape(seq_rows)
    query_pos = lax.dynamic_slice_in_dim(positions, lax.axis_index("ctx") * tok_rows, tok_rows)
    key_full, value_full = (
        lax.all_gather(key_rows, ("ctx", "tp"), axis=0, tiled=True),
        lax.all_gather(value_rows, ("ctx", "tp"), axis=0, tiled=True),
    )
    key_store = lax.dynamic_slice_in_dim(key_full, tp_rank * kv_width, kv_width, 1)
    value_store = lax.dynamic_slice_in_dim(value_full, tp_rank * kv_width, kv_width, 1)
    q_split = queries.reshape(tok_rows, kv_local, group, head_size).transpose(1, 2, 0, 3)
    do_split = cotangent.reshape(tok_rows, kv_local, group, head_size).transpose(1, 2, 0, 3)
    key_split = key_store.reshape(seq_rows, kv_local, head_size).transpose(1, 0, 2)
    value_split = value_store.reshape(seq_rows, kv_local, head_size).transpose(1, 0, 2)
    visible_all = positions[None, :] <= query_pos[:, None]

    def per_group(inputs):
        q_group, do_group, key_head, value_head = inputs

        def per_head(sums, head_inputs):
            key_grad, value_grad = sums
            q_one, do_one = head_inputs
            scores = jnp.dot(q_one, key_head.T, preferred_element_type=jnp.float32) * scale
            scores = jnp.where(visible_all, scores, NEG)
            top_score = jnp.max(scores, axis=1, keepdims=True)
            totals = jnp.sum(
                jnp.where(visible_all, jnp.exp(scores - top_score), 0.0), axis=1, keepdims=True
            )
            log_total = top_score + jnp.log(totals)
            probs = jnp.where(visible_all, jnp.exp(scores - log_total), 0.0)
            probs_low = probs.astype(jnp.bfloat16)
            attended = jnp.dot(probs_low, value_head, preferred_element_type=jnp.float32)
            delta = jnp.sum(do_one.astype(jnp.float32) * attended, axis=1, keepdims=True)
            dprobs = jnp.dot(do_one, value_head.T, preferred_element_type=jnp.float32)
            dscores = (probs * (dprobs - delta)).astype(jnp.bfloat16)
            q_grad = (
                jnp.dot(dscores, key_head, preferred_element_type=jnp.float32) * scale
            ).astype(jnp.bfloat16)
            key_grad = (
                key_grad + jnp.dot(dscores.T, q_one, preferred_element_type=jnp.float32) * scale
            )
            value_grad = value_grad + jnp.dot(
                probs_low.T, do_one, preferred_element_type=jnp.float32
            )
            return ((key_grad, value_grad), (attended.astype(jnp.bfloat16), q_grad))

        zero_rows = jnp.zeros((seq_rows, head_size), jnp.float32)
        (key_grad, value_grad), (attended, q_grad) = lax.scan(
            per_head, (zero_rows, zero_rows), (q_group, do_group)
        )
        return (attended, q_grad, key_grad, value_grad)

    attended, q_grad, key_grad, value_grad = lax.map(
        per_group, (q_split, do_split, key_split, value_split)
    )
    attended_flat = attended.transpose(2, 0, 1, 3).reshape(tok_rows, heads_local * head_size)
    q_grad_flat = q_grad.transpose(2, 0, 1, 3).reshape(tok_rows, heads_local * head_size)
    key_terms = key_grad.transpose(1, 0, 2).reshape(seq_rows, kv_width)
    value_terms = value_grad.transpose(1, 0, 2).reshape(seq_rows, kv_width)
    grad_terms = jnp.concatenate([key_terms, value_terms], axis=1)
    own_grads = lax.psum_scatter(grad_terms, "ctx", scatter_dimension=0, tiled=True)
    key_part = own_grads[:, :kv_width]
    value_part = own_grads[:, kv_width:]
    k_grad_tokens, v_grad_tokens = (
        lax.all_to_all(key_part, "tp", split_axis=0, concat_axis=1, tiled=True),
        lax.all_to_all(value_part, "tp", split_axis=0, concat_axis=1, tiled=True),
    )
    return (attended_flat[None], q_grad_flat[None], k_grad_tokens[None], v_grad_tokens[None])


def solution(mesh):
    in_specs = (
        P(),
        P(),
        P("section", None, "ctx", "tp"),
        P("section", None, ("ctx", "tp"), None),
        P("section", None, ("ctx", "tp"), None),
        P("section", "ctx", "tp"),
    )
    out_specs = (
        P("section", "ctx", "tp"),
        P("section", "ctx", "tp"),
        P("section", ("ctx", "tp"), None),
        P("section", ("ctx", "tp"), None),
    )
    return jax.shard_map(body, mesh=mesh, in_specs=in_specs, out_specs=out_specs, check_vma=False)
```

profile of v0, /device:TPU:1, one launch (start us, length us, event | category | flops | bytes accessed | tf_op | source)
XLA Modules:
  0.0 454.2 jit_solution(15236497514800470888)
XLA Ops:
  7.2 4.8 %collective-permute-start.3 = (bf16[2,22,1024]{2,0,1:T(2,128)(2,1)}, bf16[2,22,1024]{2,0,1:T(2,128)(2,1)S(1)}, u32[]{:S(2)}, u32[]{:S(2)}) collective-permute-start(bf16[2,22,1024]{2,0,1:T(2,128)(2,1)} %bitcast.117), channel_id=1, source_target_pairs={{448,0},{0,64},{64,128},{128,192},{192,256},{256,320},{320,384},{3... | collective-permute-start | bytes 270344 | tf_op jit(solution)/shard_map/ppermute | solution.py:13
  15.2 6.0 %collective-permute-done.3 = bf16[2,22,1024]{2,0,1:T(2,128)(2,1)S(1)} collective-permute-done((bf16[2,22,1024]{2,0,1:T(2,128)(2,1)}, bf16[2,22,1024]{2,0,1:T(2,128)(2,1)S(1)}, u32[]{:S(2)}, u32[]{:S(2)}) %collective-permute-start.3) | collective-permute-done | bytes 90144 | tf_op jit(solution)/shard_map/ppermute | solution.py:13
  22.0 1.9 collective-permute-start.1
  24.0 4.8 %collective-permute-done.1 = bf16[2,22,1024]{2,0,1:T(2,128)(2,1)S(1)} collective-permute-done((bf16[2,22,1024]{2,0,1:T(2,128)(2,1)}, bf16[2,22,1024]{2,0,1:T(2,128)(2,1)S(1)}, u32[]{:S(2)}, u32[]{:S(2)}) %collective-permute-start.1) | collective-permute-done | bytes 90144 | tf_op jit(solution)/shard_map/ppermute | solution.py:13
  29.5 1.9 collective-permute-start
  31.5 4.6 %collective-permute-start.2 = (bf16[176,1024]{1,0:T(8,128)(2,1)}, bf16[176,1024]{1,0:T(8,128)(2,1)S(1)}, u32[]{:S(2)}, u32[]{:S(2)}) collective-permute-start(bf16[176,1024]{1,0:T(8,128)(2,1)} %bitcast.116), channel_id=1, source_target_pairs={{64,0},{128,64},{192,128},{256,192},{320,256},{384,320},{448,384},... | collective-permute-start | bytes 1081352 | tf_op jit(solution)/shard_map/ppermute | solution.py:13
  37.0 4.4 collective-permute-done.2
  42.3 5.9 %collective-permute-done = bf16[2,176,1024]{2,1,0:T(8,128)(2,1)S(1)} collective-permute-done((bf16[2,176,1024]{2,1,0:T(8,128)(2,1)}, bf16[2,176,1024]{2,1,0:T(8,128)(2,1)S(1)}, u32[]{:S(2)}, u32[]{:S(2)}) %collective-permute-start) | collective-permute-done | bytes 720928 | tf_op jit(solution)/shard_map/ppermute | solution.py:13
  49.0 92.7 %all-gather.7.cloned.1.call-done = bf16[1,1408,1024]{2,0,1:T(2,128)(2,1)} async-done(((bf16[1,22,1024]{2,0,1:T(2,128)(2,1)}), bf16[1,1408,1024]{2,0,1:T(2,128)(2,1)}) %all-gather.7.cloned.1.call-update) | async-done | bytes 2883600 | tf_op jit(solution)/shard_map/all_gather | solution.py:42
  141.7 1.8 constant_dynamic-slice_fusion
  143.5 118.6 %all-gather.5.cloned.1.call-done = bf16[1,1408,1024]{2,0,1:T(2,128)(2,1)} async-done(((bf16[1,22,1024]{2,0,1:T(2,128)(2,1)}), bf16[1,1408,1024]{2,0,1:T(2,128)(2,1)}) %all-gather.5.cloned.1.call-update) | async-done | bytes 2883600 | tf_op jit(solution)/shard_map/all_gather | solution.py:41
  262.2 1.8 constant_dynamic-slice_fusion.2
  264.0 68.6 %while.30 = (s32[]{:T(128)}, f32[1408,128]{1,0:T(8,128)S(1)}, f32[1408,128]{1,0:T(8,128)S(1)}, bf16[8,176,128]{2,1,0:T(8,128)(2,1)}, bf16[8,176,128]{2,1,0:T(8,1...) while((s32[]{:T(128)}, f32[1408,128]{1,0:T(8,128)S(1)}, ...), condition=%wide.region_4.5_spmd.clone, body=%wide.region_0.4_spmd.clone.sunk | while | flops 386129568 | bytes 11705100 | solution.py:83
  276.8 1.4 fusion.65
  285.4 1.4 fusion.65
  294.0 1.4 fusion.65
  311.1 1.4 fusion.65
  319.7 1.4 fusion.65
  328.3 1.4 fusion.65
  333.8 89.6 %reduce-scatter.2.cloned.1.call-done = f32[176,256]{1,0:T(8,128)} async-done(((f32[1408,256]{1,0:T(8,128)}), f32[176,256]{1,0:T(8,128)}) %reduce-scatter.2.cloned.1.call-update) | async-done | bytes 180240 | tf_op jit(solution)/shard_map/reduce_scatter | solution.py:96
  425.0 7.0 %all-to-all-start = ((f32[8,22,128]{2,1,0:T(8,128)}), f32[8,22,128]{2,1,0:T(8,128)S(1)}, u32[]{:S(2)}, u32[]{:S(2)}) async-start(f32[8,22,128]{2,1,0:T(8,128)} %all_to_all.24), calls=%async_computation.1 | async-start | bytes 196608 | tf_op jit(solution)/shard_map/all_to_all | solution.py:100
  432.6 4.8 %all-to-all-done = f32[8,22,128]{2,1,0:T(8,128)S(1)} async-done(((f32[8,22,128]{2,1,0:T(8,128)}), f32[8,22,128]{2,1,0:T(8,128)S(1)}, u32[]{:S(2)}, u32[]{:S(2)}) %all-to-all-start) | async-done | bytes 90144 | tf_op jit(solution)/shard_map/all_to_all | solution.py:100
  437.4 4.2 all-to-all-start.1
  445.2 1.8 all-to-all-done.1
  (110 shorter events, 73.2 us)
Async XLA Ops:
  7.2 134.5 %all-gather.7.cloned.1.call-start = ((), (), s32[]{:S(2)}) async-start(), calls=%async_computation.5 | async-start | bytes 5857280 | tf_op jit(solution)/shard_map/all_gather | solution.py:42
  7.2 14.0 %collective-permute-start.3 = (bf16[2,22,1024]{2,0,1:T(2,128)(2,1)}, bf16[2,22,1024]{2,0,1:T(2,128)(2,1)S(1)}, u32[]{:S(2)}, u32[]{:S(2)}) collective-permute-start(bf16[2,22,1024]{2,0,1:T(2,128)(2,1)} %bitcast.117), channel_id=1, source_target_pairs={{448,0},{0,64},{64,128},{128,192},{192,256},{256,320},{320,384},{3... | collective-permute-start | bytes 270344 | tf_op jit(solution)/shard_map/ppermute | solution.py:13
  22.0 240.2 %all-gather.5.cloned.1.call-start = ((), (), s32[]{:S(2)}) async-start(), calls=%async_computation.4 | async-start | bytes 5857280 | tf_op jit(solution)/shard_map/all_gather | solution.py:41
  22.0 6.7 %collective-permute-start.1 = (bf16[2,22,1024]{2,0,1:T(2,128)(2,1)}, bf16[2,22,1024]{2,0,1:T(2,128)(2,1)S(1)}, u32[]{:S(2)}, u32[]{:S(2)}) collective-permute-start(bf16[2,22,1024]{2,0,1:T(2,128)(2,1)} %bitcast.118), channel_id=1, source_target_pairs={{448,0},{0,64},{64,128},{128,192},{192,256},{256,320},{320,384},{3... | collective-permute-start | bytes 270344 | tf_op jit(solution)/shard_map/ppermute | solution.py:13
  29.5 393.9 %reduce-scatter.2.cloned.1.call-start = ((), (), s32[]{:S(2)}) async-start(), calls=%async_computation.3 | async-start | bytes 1622016 | tf_op jit(solution)/shard_map/reduce_scatter | solution.py:96
  29.5 18.6 %collective-permute-start = (bf16[2,176,1024]{2,1,0:T(8,128)(2,1)}, bf16[2,176,1024]{2,1,0:T(8,128)(2,1)S(1)}, u32[]{:S(2)}, u32[]{:S(2)}) collective-permute-start(bf16[2,176,1024]{2,1,0:T(8,128)(2,1)} %bitcast.115), channel_id=1, source_target_pairs={{448,0},{0,64},{64,128},{128,192},{192,256},{256,320},{320,384},{3... | collective-permute-start | bytes 2162696 | tf_op jit(solution)/shard_map/ppermute | solution.py:13
  31.5 10.0 %collective-permute-start.2 = (bf16[176,1024]{1,0:T(8,128)(2,1)}, bf16[176,1024]{1,0:T(8,128)(2,1)S(1)}, u32[]{:S(2)}, u32[]{:S(2)}) collective-permute-start(bf16[176,1024]{1,0:T(8,128)(2,1)} %bitcast.116), channel_id=1, source_target_pairs={{64,0},{128,64},{192,128},{256,192},{320,256},{384,320},{448,384},... | collective-permute-start | bytes 1081352 | tf_op jit(solution)/shard_map/ppermute | solution.py:13
  332.6 111.0 %copy-start = (bf16[8,176,128]{2,1,0:T(8,128)(2,1)S(1)}, bf16[8,176,128]{2,1,0:T(8,128)(2,1)}, u32[]{:S(2)}) copy-start(bf16[8,176,128]{2,1,0:T(8,128)(2,1)} %get-tuple-element.90) | copy-start | bytes 1081348
  425.0 12.4 %all-to-all-start = ((f32[8,22,128]{2,1,0:T(8,128)}), f32[8,22,128]{2,1,0:T(8,128)S(1)}, u32[]{:S(2)}, u32[]{:S(2)}) async-start(f32[8,22,128]{2,1,0:T(8,128)} %all_to_all.24), calls=%async_computation.1 | async-start | bytes 196608 | tf_op jit(solution)/shard_map/all_to_all | solution.py:100
  437.4 9.6 %all-to-all-start.1 = ((f32[8,22,128]{2,1,0:T(8,128)}), f32[8,22,128]{2,1,0:T(8,128)S(1)}, u32[]{:S(2)}, u32[]{:S(2)}) async-start(f32[8,22,128]{2,1,0:T(8,128)} %all_to_all.27), calls=%async_computation.2 | async-start | bytes 196608 | tf_op jit(solution)/shard_map/all_to_all | solution.py:101
Sparse Core Ops, SparseCore 0:
  22.1 119.5 all-gather.6
  144.4 117.6 all-gather.4
  334.0 89.4 reduce-scatter.1
where the time goes:
time: 457 us; the launch traced here: 454 us
  waiting for transfers between devices  329 us (72%)
  matrix products  57.9 us (13%)
  starting transfers between devices  24.5 us (5%)
  local copies, waits for them, and re-layouts  19.7 us (4%)
  between operations  15.8 us (3%)
  other arithmetic  7.34 us (2%)
    all_gather x1, waiting for transfers between devices, body(): lax.all_gather(key_rows, ('ctx', 'tp'), axis=0, tiled=True)  119 us
    all_gather x1, waiting for transfers between devices, body(): lax.all_gather(value_rows, ('ctx', 'tp'), axis=0, tiled=True)  92.7 us
    reduce_scatter x1, waiting for transfers between devices, body(): lax.psum_scatter(grad_terms, 'ctx', scatter_dimension=0, tiled=True)  89.6 us
    ppermute x4, waiting for transfers between devices, passed_along(): return lax.ppermute(block, axis, route)  21.1 us
    ppermute x4, starting transfers between devices, passed_along(): return lax.ppermute(block, axis, route)  13.2 us
    dot_general x8, matrix products, per_head(): jnp.dot(dscores.T, q_one, preferred_element_type=jnp.float32) * scale  11.2 us
    dot_general x8, matrix products, per_head(): jnp.dot(probs_low.T, do_one, preferred_element_type=jnp.float32)  11 us
    dot_general x8, matrix products, per_head(): jnp.dot(q_one, key_head.T, preferred_element_type=jnp.float32) * scale  9.57 us
  transfers between devices with their start and end apart: 9, of which 9 were waited for; matrix products, arithmetic and copies ran while one was open for 2% of the time, Pallas kernels for 0%

commit v1 on v0

--- a/solution.py
+++ b/solution.py
@@ -5,6 +5,18 @@
 
 HEAD_DIM = 128
 NEG = -1e30
+
+
+def assign_group(point):
+    return jnp.concatenate(
+        jax.lax.all_to_all(
+            jnp.stack([point] * jax.lax.axis_size(("ctx", "tp")), 0),
+            axis_name=("ctx", "tp"),
+            split_axis=0,
+            concat_axis=0,
+        ),
+        axis=0,
+    )
 
 
 def passed_along(block, axis, distance):
@@ -38,7 +50,7 @@
     ).reshape(seq_rows)
     query_pos = lax.dynamic_slice_in_dim(positions, lax.axis_index("ctx") * tok_rows, tok_rows)
     key_full, value_full = (
-        lax.all_gather(key_rows, ("ctx", "tp"), axis=0, tiled=True),
+        assign_group(key_rows),
         lax.all_gather(value_rows, ("ctx", "tp"), axis=0, tiled=True),
     )
     key_store = lax.dynamic_slice_in_dim(key_full, tp_rank * kv_width, kv_width, 1)

time: 457 us -> 375 us (0.82)
  waiting for transfers between devices: 329 us -> 229 us
  starting transfers between devices: 24.5 us -> 36.1 us
  local copies, waits for them, and re-layouts: 19.7 us -> 26.5 us
    all_gather x1 -> x0, waiting for transfers between devices: 119 us -> none  [body(): lax.all_gather(key_rows, ('ctx', 'tp'), axis=0, tiled=True)]
    all_to_all x0 -> x1, waiting for transfers between devices: none -> 56.5 us  [assign_group(): jax.lax.all_to_all(jnp.stack([point] * jax.lax.axis_size(('ctx', 'tp')),...]
    all_gather x1, waiting for transfers between devices: 92.7 us -> 54.1 us  [body(): lax.all_gather(value_rows, ('ctx', 'tp'), axis=0, tiled=True)]
    all_to_all x0 -> x1, starting transfers between devices: none -> 11.7 us  [assign_group(): jax.lax.all_to_all(jnp.stack([point] * jax.lax.axis_size(('ctx', 'tp')),...]
    reshape x0 -> x1, local copies, waits for them, and re-layouts: none -> 5.36 us  [assign_group(): jnp.concatenate(jax.lax.all_to_all(jnp.stack([point] * jax.lax.axis_size(...]
  transfers between devices with their start and end apart: 9 -> 9, of which waited for: 9 -> 9; matrix products, arithmetic and copies ran while one was open for 2% -> 4% of each run, Pallas kernels for 0% -> 0%
where the time goes in v1:
time: 375 us; the launch traced here: 372 us
  waiting for transfers between devices  229 us (61%)
  matrix products  57.9 us (15%)
  starting transfers between devices  36.1 us (10%)
  local copies, waits for them, and re-layouts  26.5 us (7%)
  between operations  16.2 us (4%)
  other arithmetic  6.67 us (2%)
    reduce_scatter x1, waiting for transfers between devices, body(): lax.psum_scatter(grad_terms, 'ctx', scatter_dimension=0, tiled=True)  88.6 us
    all_to_all x1, waiting for transfers between devices, assign_group(): jax.lax.all_to_all(jnp.stack([point] * jax.lax.axis_size(('ctx', 'tp')),...  56.5 us
    all_gather x1, waiting for transfers between devices, body(): lax.all_gather(value_rows, ('ctx', 'tp'), axis=0, tiled=True)  54.1 us
    ppermute x4, waiting for transfers between devices, passed_along(): return lax.ppermute(block, axis, route)  22.9 us
    ppermute x4, starting transfers between devices, passed_along(): return lax.ppermute(block, axis, route)  13.2 us
    all_to_all x1, starting transfers between devices, assign_group(): jax.lax.all_to_all(jnp.stack([point] * jax.lax.axis_size(('ctx', 'tp')),...  11.7 us
    dot_general x8, matrix products, per_head(): jnp.dot(dscores.T, q_one, preferred_element_type=jnp.float32) * scale  11.2 us
    dot_general x8, matrix products, per_head(): jnp.dot(probs_low.T, do_one, preferred_element_type=jnp.float32)  11 us
  transfers between devices with their start and end apart: 9, of which 9 were waited for; matrix products, arithmetic and copies ran while one was open for 4% of the time, Pallas kernels for 0%

profile of v1, /device:TPU:1, one launch (start us, length us, event | category | flops | bytes accessed | tf_op | source)
XLA Modules:
  0.0 372.2 jit_solution(74936306192800214)
XLA Ops:
  8.1 4.8 %collective-permute-start.1 = (bf16[2,22,1024]{2,1,0:T(8,128)(2,1)S(1)}, bf16[2,22,1024]{2,1,0:T(8,128)(2,1)S(1)}, u32[]{:S(2)}, u32[]{:S(2)}) collective-permute-start(bf16[2,22,1024]{2,1,0:T(8,128)(2,1)S(1)} %bitcast.112), channel_id=1, source_target_pairs={{448,0},{0,64},{64,128},{128,192},{192,256},{256,320},{320,384},{3... | collective-permute-start | bytes 270344 | tf_op jit(solution)/shard_map/ppermute | solution.py:25
  16.1 6.0 %collective-permute-done.1 = bf16[2,22,1024]{2,1,0:T(8,128)(2,1)S(1)} collective-permute-done((bf16[2,22,1024]{2,1,0:T(8,128)(2,1)S(1)}, bf16[2,22,1024]{2,1,0:T(8,128)(2,1)S(1)}, u32[]{:S(2)}, u32[]{:S(2)}) %collective-permute-start.1) | collective-permute-done | bytes 90144 | tf_op jit(solution)/shard_map/ppermute | solution.py:25
  22.1 2.0 stack.2
  24.1 11.7 %all-to-all-start = ((bf16[64,22,1024]{2,1,0:T(8,128)(2,1)}), bf16[64,22,1024]{2,1,0:T(8,128)(2,1)}, u32[]{:S(2)}, u32[]{:S(2)}) async-start(bf16[64,22,1024]{2,1,0:T(8,128)(2,1)} %stack.2), calls=%async_computation | async-start | bytes 6291456 | tf_op jit(solution)/shard_map/all_to_all | solution.py:12
  35.8 1.9 collective-permute-start.3
  37.8 5.0 %collective-permute-done.3 = bf16[2,22,1024]{2,0,1:T(2,128)(2,1)S(1)} collective-permute-done((bf16[2,22,1024]{2,0,1:T(2,128)(2,1)S(1)}, bf16[2,22,1024]{2,0,1:T(2,128)(2,1)S(1)}, u32[]{:S(2)}, u32[]{:S(2)}) %collective-permute-start.3) | collective-permute-done | bytes 90144 | tf_op jit(solution)/shard_map/ppermute | solution.py:25
  43.5 1.9 collective-permute-start
  45.5 4.6 %collective-permute-start.2 = (bf16[176,1024]{1,0:T(8,128)(2,1)}, bf16[176,1024]{1,0:T(8,128)(2,1)S(1)}, u32[]{:S(2)}, u32[]{:S(2)}) collective-permute-start(bf16[176,1024]{1,0:T(8,128)(2,1)} %bitcast.6), channel_id=1, source_target_pairs={{64,0},{128,64},{192,128},{256,192},{320,256},{384,320},{448,384},... | collective-permute-start | bytes 1081352 | tf_op jit(solution)/shard_map/ppermute | solution.py:25
  50.4 6.2 %collective-permute-done.2 = bf16[176,1024]{1,0:T(8,128)(2,1)S(1)} collective-permute-done((bf16[176,1024]{1,0:T(8,128)(2,1)}, bf16[176,1024]{1,0:T(8,128)(2,1)S(1)}, u32[]{:S(2)}, u32[]{:S(2)}) %collective-permute-start.2) | collective-permute-done | bytes 360480 | tf_op jit(solution)/shard_map/ppermute | solution.py:25
  57.4 5.7 %collective-permute-done = bf16[2,176,1024]{2,1,0:T(8,128)(2,1)S(1)} collective-permute-done((bf16[2,176,1024]{2,1,0:T(8,128)(2,1)S(1)}, bf16[2,176,1024]{2,1,0:T(8,128)(2,1)S(1)}, u32[]{:S(2)}, u32[]{:S(2)}) %collective-permute-start) | collective-permute-done | bytes 720928 | tf_op jit(solution)/shard_map/ppermute | solution.py:25
  64.0 56.5 %all-to-all-done = bf16[64,22,1024]{2,1,0:T(8,128)(2,1)} async-done(((bf16[64,22,1024]{2,1,0:T(8,128)(2,1)}), bf16[64,22,1024]{2,1,0:T(8,128)(2,1)}, u32[]{:S(2)}, u32[]{:S(2)}) %all-to-all-start) | async-done | bytes 2883616 | tf_op jit(solution)/shard_map/all_to_all | solution.py:12
  120.5 5.4 %reshape.64 = bf16[1408,1024]{1,0:T(8,128)(2,1)} reshape(bf16[64,22,1024]{2,1,0:T(8,128)(2,1)} %all-to-all-done) | data formatting | bytes 5767168 | tf_op jit(solution)/shard_map/reshape | solution.py:11
  126.9 54.1 %all-gather.3.cloned.1.call-done = bf16[1,1408,1024]{2,0,1:T(2,128)(2,1)} async-done(((bf16[1,22,1024]{2,0,1:T(2,128)(2,1)}), bf16[1,1408,1024]{2,0,1:T(2,128)(2,1)}) %all-gather.3.cloned.1.call-update) | async-done | bytes 2883600 | tf_op jit(solution)/shard_map/all_gather | solution.py:54
  180.9 1.8 constant_dynamic-slice_fusion
  182.8 68.6 %while.30 = (s32[]{:T(128)}, f32[1408,128]{1,0:T(8,128)S(1)}, f32[1408,128]{1,0:T(8,128)S(1)}, bf16[8,176,128]{2,1,0:T(8,128)(2,1)}, bf16[8,176,128]{2,1,0:T(8,1...) while((s32[]{:T(128)}, f32[1408,128]{1,0:T(8,128)S(1)}, ...), condition=%wide.region_4.5_spmd.clone, body=%wide.region_0.4_spmd.clone.sunk | while | flops 386129568 | bytes 11705100 | solution.py:95
  187.0 1.4 fusion.65
  195.6 1.4 fusion.65
  204.2 1.4 fusion.65
  247.0 1.4 fusion.65
  252.6 88.6 %reduce-scatter.2.cloned.1.call-done = f32[176,256]{1,0:T(8,128)} async-done(((f32[1408,256]{1,0:T(8,128)}), f32[176,256]{1,0:T(8,128)}) %reduce-scatter.2.cloned.1.call-update) | async-done | bytes 180240 | tf_op jit(solution)/shard_map/reduce_scatter | solution.py:108
  342.8 6.9 %all-to-all-start.1 = ((f32[8,22,128]{2,1,0:T(8,128)}), f32[8,22,128]{2,1,0:T(8,128)S(1)}, u32[]{:S(2)}, u32[]{:S(2)}) async-start(f32[8,22,128]{2,1,0:T(8,128)} %all_to_all.28), calls=%async_computation.2 | async-start | bytes 196608 | tf_op jit(solution)/shard_map/all_to_all | solution.py:112
  350.4 4.8 %all-to-all-done.1 = f32[8,22,128]{2,1,0:T(8,128)S(1)} async-done(((f32[8,22,128]{2,1,0:T(8,128)}), f32[8,22,128]{2,1,0:T(8,128)S(1)}, u32[]{:S(2)}, u32[]{:S(2)}) %all-to-all-start.1) | async-done | bytes 90144 | tf_op jit(solution)/shard_map/all_to_all | solution.py:112
  355.1 4.2 %all-to-all-start.2 = ((f32[8,22,128]{2,1,0:T(8,128)}), f32[8,22,128]{2,1,0:T(8,128)S(1)}, u32[]{:S(2)}, u32[]{:S(2)}) async-start(f32[8,22,128]{2,1,0:T(8,128)} %all_to_all.31), calls=%async_computation.3 | async-start | bytes 196608 | tf_op jit(solution)/shard_map/all_to_all | solution.py:113
  363.0 1.8 all-to-all-done.2
  (117 shorter events, 76.4 us)
Async XLA Ops:
  8.1 14.0 %collective-permute-start.1 = (bf16[2,22,1024]{2,1,0:T(8,128)(2,1)S(1)}, bf16[2,22,1024]{2,1,0:T(8,128)(2,1)S(1)}, u32[]{:S(2)}, u32[]{:S(2)}) collective-permute-start(bf16[2,22,1024]{2,1,0:T(8,128)(2,1)S(1)} %bitcast.112), channel_id=1, source_target_pairs={{448,0},{0,64},{64,128},{128,192},{192,256},{256,320},{320,384},{3... | collective-permute-start | bytes 270344 | tf_op jit(solution)/shard_map/ppermute | solution.py:25
  24.1 11.7 %copy-start.2 = (bf16[1,2,22,1024]{3,1,2,0:T(2,128)(2,1)S(1)}, bf16[1,2,22,1024]{3,1,2,0:T(2,128)(2,1)}, u32[]{:S(2)}) copy-start(bf16[1,2,22,1024]{3,1,2,0:T(2,128)(2,1)} %param.12) | copy-start | bytes 270340
  24.1 19.4 %copy-start.1 = (bf16[1,2,176,1024]{3,2,1,0:T(8,128)(2,1)S(1)}, bf16[1,2,176,1024]{3,2,1,0:T(8,128)(2,1)}, u32[]{:S(2)}) copy-start(bf16[1,2,176,1024]{3,2,1,0:T(8,128)(2,1)} %param.10) | copy-start | bytes 2162692
  24.1 26.0 %copy-start.3 = (s32[16]{0:T(128)S(1)}, s32[16]{0:T(128)}, u32[]{:S(2)}) copy-start(s32[16]{0:T(128)} %param.8) | copy-start | bytes 196
  24.1 96.4 %all-to-all-start = ((bf16[64,22,1024]{2,1,0:T(8,128)(2,1)}), bf16[64,22,1024]{2,1,0:T(8,128)(2,1)}, u32[]{:S(2)}, u32[]{:S(2)}) async-start(bf16[64,22,1024]{2,1,0:T(8,128)(2,1)} %stack.2), calls=%async_computation | async-start | bytes 6291456 | tf_op jit(solution)/shard_map/all_to_all | solution.py:12
  35.8 145.2 %all-gather.3.cloned.1.call-start = ((), (), s32[]{:S(2)}) async-start(), calls=%async_computation.5 | async-start | bytes 5857280 | tf_op jit(solution)/shard_map/all_gather | solution.py:54
  35.8 6.9 %collective-permute-start.3 = (bf16[2,22,1024]{2,0,1:T(2,128)(2,1)S(1)}, bf16[2,22,1024]{2,0,1:T(2,128)(2,1)S(1)}, u32[]{:S(2)}, u32[]{:S(2)}) collective-permute-start(bf16[2,22,1024]{2,0,1:T(2,128)(2,1)S(1)} %bitcast.116), channel_id=1, source_target_pairs={{448,0},{0,64},{64,128},{128,192},{192,256},{256,320},{320,384},{3... | collective-permute-start | bytes 270344 | tf_op jit(solution)/shard_map/ppermute | solution.py:25
  43.5 297.7 %reduce-scatter.2.cloned.1.call-start = ((), (), s32[]{:S(2)}) async-start(), calls=%async_computation.4 | async-start | bytes 1622016 | tf_op jit(solution)/shard_map/reduce_scatter | solution.py:108
  43.5 19.6 %collective-permute-start = (bf16[2,176,1024]{2,1,0:T(8,128)(2,1)S(1)}, bf16[2,176,1024]{2,1,0:T(8,128)(2,1)S(1)}, u32[]{:S(2)}, u32[]{:S(2)}) collective-permute-start(bf16[2,176,1024]{2,1,0:T(8,128)(2,1)S(1)} %bitcast.115), channel_id=1, source_target_pairs={{448,0},{0,64},{64,128},{128,192},{192,256},{256,320},{320,384},{3... | collective-permute-start | bytes 2162696 | tf_op jit(solution)/shard_map/ppermute | solution.py:25
  45.5 11.1 %collective-permute-start.2 = (bf16[176,1024]{1,0:T(8,128)(2,1)}, bf16[176,1024]{1,0:T(8,128)(2,1)S(1)}, u32[]{:S(2)}, u32[]{:S(2)}) collective-permute-start(bf16[176,1024]{1,0:T(8,128)(2,1)} %bitcast.6), channel_id=1, source_target_pairs={{64,0},{128,64},{192,128},{256,192},{320,256},{384,320},{448,384},... | collective-permute-start | bytes 1081352 | tf_op jit(solution)/shard_map/ppermute | solution.py:25
  251.4 109.9 %copy-start = (bf16[8,176,128]{2,1,0:T(8,128)(2,1)S(1)}, bf16[8,176,128]{2,1,0:T(8,128)(2,1)}, u32[]{:S(2)}) copy-start(bf16[8,176,128]{2,1,0:T(8,128)(2,1)} %get-tuple-element.90) | copy-start | bytes 1081348
  342.8 12.3 %all-to-all-start.1 = ((f32[8,22,128]{2,1,0:T(8,128)}), f32[8,22,128]{2,1,0:T(8,128)S(1)}, u32[]{:S(2)}, u32[]{:S(2)}) async-start(f32[8,22,128]{2,1,0:T(8,128)} %all_to_all.28), calls=%async_computation.2 | async-start | bytes 196608 | tf_op jit(solution)/shard_map/all_to_all | solution.py:112
  355.1 9.6 %all-to-all-start.2 = ((f32[8,22,128]{2,1,0:T(8,128)}), f32[8,22,128]{2,1,0:T(8,128)S(1)}, u32[]{:S(2)}, u32[]{:S(2)}) async-start(f32[8,22,128]{2,1,0:T(8,128)} %all_to_all.31), calls=%async_computation.3 | async-start | bytes 196608 | tf_op jit(solution)/shard_map/all_to_all | solution.py:113
Sparse Core Ops, SparseCore 0:
  43.6 137.2 all-gather.2
  252.7 88.4 reduce-scatter.1
